TPU v7x, 32 devices: a whole 2x2x4 slice. The times are simulated.
32 devices in a mesh: bucket: 8 (over z, x), rel: 4 (over y, core).
Axes of the slice: x: 2, y: 2, z: 4, core: 2. Of those that a mesh axis runs over, the one named last changes fastest.
Arguments:
- left_rows: float32 [8192, 512], P(('bucket', 'rel')), may hold values from -1.2 to 1.2
- left_state: float32 [8192], P(('bucket', 'rel')), may hold values from 1e-06 to 0.0001
- right_rows: float32 [8192, 512], P(('bucket', 'rel')), may hold values from -1.2 to 1.2
- right_state: float32 [8192], P(('bucket', 'rel')), may hold values from 1e-06 to 0.0001
- relations: bfloat16 [4, 512, 512], P('rel'), may hold values from -0.25 to 0.25
- fetch_ids: int32 [8, 4, 4], P('bucket', 'rel'), may hold values from 0 to 3
- edge_left: int32 [8, 4, 2, 512], P('bucket', 'rel'), may hold values from 0 to 255
- edge_right: int32 [8, 4, 2, 512], P('bucket', 'rel'), may hold values from 0 to 255
- edge_slot: int32 [8, 4, 2, 512], P('bucket', 'rel'), may hold values from 0 to 1
- edge_weight: int32 [8, 4, 2, 512], P('bucket', 'rel'), may hold values from 1 to 4
- matching: int32 [1], replicated, may hold values from 1 to 7
Outputs:
- left_out: float32 [8192, 512], P(('bucket', 'rel'))
- left_state_out: float32 [8192], P(('bucket', 'rel'))
- right_out: float32 [8192, 512], P(('bucket', 'rel'))
- right_state_out: float32 [8192], P(('bucket', 'rel'))
- rel_grad: float32 [4, 512, 512], P('rel')
Inputs may be any that keep to these rules, and one draw needn't show every extreme that they name: Bucket b is paired with bucket b XOR matching.
All inputs are finite; a program needn't handle non-finite values.
Results may differ from a plain program's by a relative error of at most 0.0015.
The roundings to bfloat16 on the way count: a program that leaves them out, or rounds other values in their place, can miss the bound.
Values may be sent and summed in bfloat16 or wider, within the bound.
No kernel may reach another device: no remote copies, remote signals or barrier semaphores. Data moves between devices by JAX's collectives and lax.ppermute only.
A program may use at most 64 MiB of HBM per device.

v0:
```python
import jax
import jax.numpy as jnp
from jax import lax
from jax.sharding import PartitionSpec as P

learn_rate = 0.1


def edge_targets(edge_left, edge_right, edge_slot, edge_weight, block_len):
    table = jnp.zeros((2, block_len, block_len), jnp.float32)
    table = table.at[edge_slot, edge_left, edge_right].add(edge_weight.astype(jnp.float32))
    return [table[0], table[1]]


def adagrad(table, state, gradient):
    state_new = state + jnp.mean(gradient * gradient, axis=1)
    return (table - learn_rate * gradient / jnp.sqrt(state_new)[:, None], state_new)


def one_round(
    left_block,
    left_st,
    right_block,
    right_st,
    rel_pair,
    edge_left,
    edge_right,
    edge_slot,
    edge_weight,
):
    block_len = left_block.shape[0]
    left_half = left_block.astype(jnp.bfloat16)
    right_half = right_block.astype(jnp.bfloat16)
    targets = edge_targets(edge_left, edge_right, edge_slot, edge_weight, block_len)
    grad_left = jnp.zeros(left_block.shape, jnp.float32)
    grad_right = jnp.zeros(right_block.shape, jnp.float32)
    rel_grads = []
    for slot_index in range(2):
        matrix = rel_pair[slot_index]
        projected = jnp.dot(left_half, matrix, preferred_element_type=jnp.float32).astype(
            jnp.bfloat16
        )
        scores = jnp.dot(projected, right_half.T, preferred_element_type=jnp.float32)
        score_grad = ((jax.nn.sigmoid(scores) - targets[slot_index]) / block_len).astype(
            jnp.bfloat16
        )
        carried = jnp.dot(score_grad, right_half, preferred_element_type=jnp.float32).astype(
            jnp.bfloat16
        )
        grad_left = grad_left + jnp.dot(carried, matrix.T, preferred_element_type=jnp.float32)
        grad_right = grad_right + jnp.dot(
            score_grad.T, projected, preferred_element_type=jnp.float32
        )
        rel_grads.append(jnp.dot(left_half.T, carried, preferred_element_type=jnp.float32))
    left_new, left_st_new = adagrad(left_block, left_st, grad_left)
    right_new, right_st_new = adagrad(right_block, right_st, grad_right)
    return (left_new, left_st_new, right_new, right_st_new, rel_grads)


def partner_blocks(row_block, state_block, switch):
    block_len = row_block.shape[0]
    width = row_block.shape[1]
    partner = jnp.bitwise_xor(lax.axis_index("bucket"), switch)
    portion = (
        lax.all_gather(row_block, "bucket", axis=0, tiled=True),
        lax.all_gather(state_block, "bucket", axis=0, tiled=True),
    )
    block_count = portion[0].shape[0] // block_len
    owners = jnp.arange(block_count, dtype=jnp.int32)
    chosen = owners == partner
    rows_part = portion[0].reshape(block_count, block_len, width)
    states_part = portion[1].reshape(block_count, block_len)
    rows_new = jnp.sum(jnp.where(chosen[:, None, None], rows_part, jnp.float32(0.0)), axis=0)
    states_new = jnp.sum(jnp.where(chosen[:, None], states_part, jnp.float32(0.0)), axis=0)
    return (rows_new, states_new)


def reduce_gradients(gradients, rel_ids, rel_total, width):
    stacked = jnp.stack(gradients)
    own_rows = rel_total // lax.axis_size("rel") * width
    rel_count_piece = own_rows * lax.axis_size("rel") // width
    rel_list = jnp.arange(rel_count_piece, dtype=jnp.int32)
    weights = (rel_ids[:, None] == rel_list[None, :]).astype(jnp.float32)
    term = jnp.einsum("sk,sde->kde", weights, stacked, precision=lax.Precision.HIGHEST)
    partial_sum = lax.psum_scatter(
        term.reshape(rel_count_piece * width, width), "rel", scatter_dimension=0, tiled=True
    )
    return lax.psum(partial_sum, "bucket")


def on_device(
    left_rows,
    left_state,
    right_rows,
    right_state,
    relations,
    fetch_ids,
    edge_left,
    edge_right,
    edge_slot,
    edge_weight,
    matching,
):
    width = relations.shape[1]
    rel_table = lax.all_gather(relations, "rel", axis=0, tiled=True)
    rel_total = rel_table.shape[0]
    rel_ids = fetch_ids[0, 0]
    switch = matching[0]
    table_left, state_left = (left_rows, left_state)
    row_block, state_block = (right_rows, right_state)
    gradients = []
    for round_index in range(2):
        rel_pair = jnp.take(rel_table, rel_ids[2 * round_index : 2 * round_index + 2], axis=0)
        table_left, state_left, row_block, state_block, rel_grads = one_round(
            table_left,
            state_left,
            row_block,
            state_block,
            rel_pair,
            edge_left[0, 0, round_index],
            edge_right[0, 0, round_index],
            edge_slot[0, 0, round_index],
            edge_weight[0, 0, round_index],
        )
        gradients.extend(rel_grads)
        if round_index == 0:
            row_block, state_block = partner_blocks(row_block, state_block, switch)
    owned = reduce_gradients(gradients, rel_ids, rel_total, width)
    return (table_left, state_left, row_block, state_block, owned.reshape(-1, width, width))


def solution(mesh):
    in_specs = (
        P(("bucket", "rel"), None),
        P(("bucket", "rel")),
        P(("bucket", "rel"), None),
        P(("bucket", "rel")),
        P("rel", None, None),
        P("bucket", "rel", None),
        P("bucket", "rel", None, None),
        P("bucket", "rel", None, None),
        P("bucket", "rel", None, None),
        P("bucket", "rel", None, None),
        P(),
    )
    out_specs = (
        P(("bucket", "rel"), None),
        P(("bucket", "rel")),
        P(("bucket", "rel"), None),
        P(("bucket", "rel")),
        P("rel", None, None),
    )
    return jax.shard_map(
        on_device, mesh=mesh, in_specs=in_specs, out_specs=out_specs, check_vma=False
    )
```

profile of v0, /device:TPU:0, one launch (start us, length us, event | category | flops | bytes accessed | tf_op | source)
XLA Modules:
  0.0 281.4 jit_solution(3566939604815437510)
XLA Ops:
  7.2 0.7 all-gather.4.cloned.1.call-update
  8.0 1.1 convert_element_type.65
  9.0 1.1 convert_element_type.63
  10.1 0.8 slice_convert_fusion
  10.9 0.8 or_select_fusion
  11.7 31.3 %scatter_fusion = f32[2,256,256]{2,1,0:T(8,128)S(1)} fusion(f32[2,256,256]{2,1,0:T(8,128)S(1)} %broadcast.145.clone, s32[512]{0:T(512)S(1)} %bitcast.126, f32[512]{0:T(512)S(1)} %bitcast.131), kind=kCustom, calls=%fused_computation.2 | custom fusion | flops 512 | bytes 12288 | tf_op jit(solution)/shard_map/scatter-add | solution.py:11
  43.1 0.6 compare_and_fusion
  43.7 2.2 gather_fusion
  48.6 0.9 divide_subtract_fusion.2
  50.5 31.3 %scatter_fusion.1 = f32[2,256,256]{2,1,0:T(8,128)S(1)} fusion(f32[2,256,256]{2,1,0:T(8,128)S(1)} %broadcast.145.clone.1, s32[512]{0:T(512)S(1)} %bitcast.125, f32[512]{0:T(512)S(1)} %bitcast.130), kind=kCustom, calls=%fused_computation.3 | custom fusion | flops 512 | bytes 12288 | tf_op jit(solution)/shard_map/scatter-add | solution.py:11
  82.3 3.2 %gather_fusion.1 = bf16[2,512,512]{2,1,0:T(8,128)(2,1)} fusion(bf16[4,512,512]{2,1,0:T(8,128)(2,1)} %all-gather.4.cloned.1.call-done, s32[1024]{0:T(1024)S(1)} %get-tuple-element.30), kind=kCustom, calls=%fused_computation.1.clone | custom fusion | bytes 2097160 | tf_op jit(solution)/shard_map/jit(_take)/gather | solution.py:113
  85.8 1.3 convolution_bitcast_fusion.2
  87.3 1.3 convolution_bitcast_fusion.3
  90.0 1.0 convolution_convert_fusion.3
  91.1 34.1 %all-gather.6.cloned.1.call-done = f32[2048,512]{1,0:T(8,128)} async-done(((f32[256,512]{1,0:T(8,128)}), f32[2048,512]{1,0:T(8,128)}) %all-gather.6.cloned.1.call-update) | async-done | bytes 4194320 | tf_op jit(solution)/shard_map/all_gather | solution.py:65
  125.2 2.9 %select_reduce_fusion = f32[256,512]{1,0:T(8,128)S(1)} fusion(f32[8,256,512]{2,1,0:T(8,128)} %bitcast.128, pred[8]{0:T(512)(128)(4,1)S(1)} %copy-done.14), kind=kLoop, calls=%fused_computation.5 | loop fusion | flops 1966080 | bytes 4718600 | tf_op jit(solution)/shard_map/reduce_sum | solution.py:73
  130.3 2.4 pad_maximum_fusion
  132.7 5.5 %copy.25 = f32[4,512,512]{2,0,1:T(4,128)} copy(f32[4,512,512]{1,2,0:T(8,128)} %pad_maximum_fusion) | data formatting | bytes 8388608 | tf_op jit(solution)/shard_map/stack | solution.py:79
  138.2 6.2 %fusion.32 = f32[4,512,512]{2,0,1:T(4,128)S(1)} fusion(f32[4,512,512]{2,0,1:T(4,128)} %copy.25, s32[4]{0:T(128)S(1)} %bitcast.132), kind=kOutput, calls=%fused_computation.98 | convolution fusion | flops 50331664 | bytes 8388624 | tf_op jit(solution)/shard_map/sk,sde->kde/dot_general | solution.py:84
  144.4 3.2 %copy.26 = f32[4,512,512]{2,1,0:T(8,128)} copy(f32[4,512,512]{2,0,1:T(4,128)S(1)} %fusion.32) | data formatting | bytes 8388608 | tf_op jit(solution)/shard_map/sk,sde->kde/dot_general | solution.py:84
  147.7 0.6 copy-done.13
  148.3 18.1 %all-gather = f32[8,1,256]{2,1,0:T(1,128)S(1)} all-gather(f32[1,1,256]{2,1,0:T(1,128)S(1)} %bitcast.133), channel_id=1, replica_groups=mesh['bucket'=8,'rel'=4] {'bucket'}, dimensions={0}, use_global_device_ids=true | all-gather | bytes 9216 | tf_op jit(solution)/shard_map/all_gather | solution.py:66
  166.5 1.2 fusion.41
  167.7 1.1 fusion.25
  168.9 2.0 multiply_reduce_fusion
  170.9 20.1 %reduce-scatter.2.cloned.1.call-done = f32[512,512]{1,0:T(8,128)} async-done(((f32[2048,512]{1,0:T(8,128)}), f32[512,512]{1,0:T(8,128)}) %reduce-scatter.2.cloned.1.call-update) | async-done | bytes 1048592 | tf_op jit(solution)/shard_map/reduce_scatter | solution.py:85
  191.6 1.5 multiply_reduce_fusion.1
  193.0 0.6 fusion.38
  193.6 2.0 divide_subtract_fusion
  195.5 1.0 divide_subtract_fusion.1
  196.6 76.1 %all-reduce.2.cloned.1.call-done = f32[1,512,512]{2,1,0:T(8,128)} async-done(((f32[1,512,512]{2,1,0:T(8,128)}), f32[1,512,512]{2,1,0:T(8,128)}) %all-reduce.2.cloned.1.call-update) | async-done | bytes 1048592 | tf_op jit(solution)/shard_map/psum | solution.py:88
  272.6 2.3 copy.35
  (72 shorter events, 8.3 us)
Async XLA Ops:
  7.2 35.9 %copy-start.11 = (s32[1,1,4]{2,1,0:T(1,128)S(1)}, s32[1,1,4]{2,1,0:T(1,128)}, u32[]{:S(2)}) copy-start(s32[1,1,4]{2,1,0:T(1,128)} %param.18) | copy-start | bytes 52
  7.2 36.5 %all-gather.4.cloned.1.call-start = ((), (), s32[]{:S(2)}) async-start(), calls=%async_computation.1 | async-start | bytes 2621440 | tf_op jit(solution)/shard_map/all_gather | solution.py:105
  7.9 117.3 %all-gather.6.cloned.1.call-start = ((), (), s32[]{:S(2)}) async-start(), calls=%async_computation.2 | async-start | bytes 4718592 | tf_op jit(solution)/shard_map/all_gather | solution.py:65
  46.1 2.0 copy-start.17
  46.1 2.5 copy-start.6
  49.6 141.4 %reduce-scatter.2.cloned.1.call-start = ((), (), s32[]{:S(2)}) async-start(), calls=%async_computation.3 | async-start | bytes 5242880 | tf_op jit(solution)/shard_map/reduce_scatter | solution.py:85
  85.5 3.9 %copy-start.12 = (f32[256]{0:T(256)S(1)}, f32[256]{0:T(256)}, u32[]{:S(2)}) copy-start(f32[256]{0:T(256)} %param.14) | copy-start | bytes 3076
  85.5 3.9 %copy-start = (f32[256,512]{1,0:T(8,128)S(1)}, f32[256,512]{1,0:T(8,128)}, u32[]{:S(2)}) copy-start(f32[256,512]{1,0:T(8,128)} %param.13) | copy-start | bytes 1572868
  85.7 3.8 %copy-start.1 = (bf16[2,512,512]{2,1,0:T(8,128)(2,1)S(1)}, bf16[2,512,512]{2,1,0:T(8,128)(2,1)}, u32[]{:S(2)}) copy-start(bf16[2,512,512]{2,1,0:T(8,128)(2,1)} %gather_fusion.1) | copy-start | bytes 3145732
  85.8 3.8 %copy-start.16 = (pred[2]{0:T(512)(128)(4,1)S(1)}, pred[2]{0:T(512)(128)(4,1)}, u32[]{:S(2)}) copy-start(pred[2]{0:T(512)(128)(4,1)} %get-tuple-element.12) | copy-start | bytes 10
  88.6 36.6 %copy-start.14 = (pred[8]{0:T(512)(128)(4,1)S(1)}, pred[8]{0:T(512)(128)(4,1)}, u32[]{:S(2)}) copy-start(pred[8]{0:T(512)(128)(4,1)} %iota_compare_fusion.1) | copy-start | bytes 28
  89.5 35.7 %copy-start.4 = (bf16[256,512]{1,0:T(8,128)(2,1)}, bf16[256,512]{1,0:T(8,128)(2,1)S(1)}, u32[]{:S(2)}) copy-start(bf16[256,512]{1,0:T(8,128)(2,1)S(1)} %fusion.36) | copy-start | bytes 786436
  90.0 38.1 %copy-start.9 = (bf16[256,512]{1,0:T(8,128)(2,1)}, bf16[256,512]{1,0:T(8,128)(2,1)S(1)}, u32[]{:S(2)}) copy-start(bf16[256,512]{1,0:T(8,128)(2,1)S(1)} %convolution_convert_fusion.1) | copy-start | bytes 786436
  125.2 3.5 %copy-start.10 = (bf16[256,512]{1,0:T(8,128)(2,1)S(1)}, bf16[256,512]{1,0:T(8,128)(2,1)}, u32[]{:S(2)}) copy-start(bf16[256,512]{1,0:T(8,128)(2,1)} %convolution_convert_fusion.3) | copy-start | bytes 786436
  125.2 4.4 %copy-start.5 = (bf16[256,512]{1,0:T(8,128)(2,1)S(1)}, bf16[256,512]{1,0:T(8,128)(2,1)}, u32[]{:S(2)}) copy-start(bf16[256,512]{1,0:T(8,128)(2,1)} %copy-done.4) | copy-start | bytes 786436
  128.1 2.3 copy-start.2
  128.1 2.3 copy-start.3
  129.0 0.7 copy-start.7
  147.7 0.7 copy-start.13
  147.7 18.8 %copy-start.15 = (pred[8]{0:T(512)(128)(4,1)S(1)}, pred[8]{0:T(512)(128)(4,1)}, u32[]{:S(2)}) copy-start(pred[8]{0:T(512)(128)(4,1)} %iota_compare_fusion.1) | copy-start | bytes 28
  147.7 18.9 %copy-start.8 = (bf16[256,256]{1,0:T(8,128)(2,1)S(1)}, bf16[256,256]{1,0:T(8,128)(2,1)}, u32[]{:S(2)}) copy-start(bf16[256,256]{1,0:T(8,128)(2,1)} %copy-done.7) | copy-start | bytes 393220
  147.7 124.9 %all-reduce.2.cloned.1.call-start = ((), (), s32[]{:S(2)}) async-start(), calls=%async_computation.4 | async-start | bytes 2097152 | tf_op jit(solution)/shard_map/psum | solution.py:88
Sparse Core Ops, SparseCore 0:
  9.5 25.2 all-gather.3
  49.7 75.4 all-gather.5
  147.8 43.1 reduce-scatter.1
  194.3 78.2 all-reduce.1
where the time goes:
time: 282 us; the launch traced here: 281 us
  waiting for transfers between devices  131 us (46%)
  other arithmetic  79 us (28%)
  matrix products  20.7 us (7%)
  blocking collectives  18.1 us (6%)
  local copies, waits for them, and re-layouts  17.5 us (6%)
  between operations  14.8 us (5%)
    psum x1, waiting for transfers between devices, reduce_gradients(): return lax.psum(partial_sum, 'bucket')  76.1 us
    scatter-add x2, other arithmetic, edge_targets(): table.at[edge_slot, edge_left, edge_right]  62.7 us
    all_gather x1, waiting for transfers between devices, partner_blocks(): lax.all_gather(row_block, 'bucket', axis=0, tiled=True)  34.1 us
    reduce_scatter x1, waiting for transfers between devices, reduce_gradients(): lax.psum_scatter(term.reshape(rel_count_piece * width, width), 'rel', sca...  20.1 us
    all_gather x1, blocking collectives, partner_blocks(): lax.all_gather(state_block, 'bucket', axis=0, tiled=True)  18.1 us
    dot_general x1, matrix products, reduce_gradients(): jnp.einsum('sk,sde->kde', weights, stacked, precision=lax.Precision.HIGHEST)  6.2 us
  transfers between devices with their start and end apart: 4, of which 3 were waited for; matrix products, arithmetic and copies ran while one was open for 31% of the time, Pallas kernels for 0%

commit v1 on v0

--- a/solution.py
+++ b/solution.py
@@ -85,7 +85,7 @@
     partial_sum = lax.psum_scatter(
         term.reshape(rel_count_piece * width, width), "rel", scatter_dimension=0, tiled=True
     )
-    return lax.psum(partial_sum, "bucket")
+    return jnp.sum(lax.all_gather(partial_sum, "bucket"), axis=0)
 
 
 def on_device(

time: 282 us -> 330 us (1.17)
  waiting for transfers between devices: 131 us -> 177 us
  other arithmetic: 79 us -> 83.5 us
  local copies, waits for them, and re-layouts: 17.5 us -> 14.2 us
    all_gather x0 -> x1, waiting for transfers between devices: none -> 98.9 us  [reduce_gradients(): return jnp.sum(lax.all_gather(partial_sum, 'bucket'), axis=0)]
    psum x1 -> x0, waiting for transfers between devices: 76.1 us -> none  [reduce_gradients(): return lax.psum(partial_sum, 'bucket')]
    reduce_scatter x1, waiting for transfers between devices: 20.1 us -> 43.2 us  [reduce_gradients(): lax.psum_scatter(term.reshape(rel_count_piece * width, width), 'rel', sca...]
    reduce_sum x0 -> x1, other arithmetic: none -> 5.46 us  [reduce_gradients(): return jnp.sum(lax.all_gather(partial_sum, 'bucket'), axis=0)]
  transfers between devices with their start and end apart: 4 -> 4, of which waited for: 3 -> 3; matrix products, arithmetic and copies ran while one was open for 31% -> 25% of each run, Pallas kernels for 0% -> 0%
where the time goes in v1:
time: 330 us; the launch traced here: 329 us
  waiting for transfers between devices  177 us (54%)
  other arithmetic  83.5 us (25%)
  blocking collectives  21.1 us (6%)
  matrix products  18.1 us (5%)
  between operations  14.8 us (4%)
  local copies, waits for them, and re-layouts  14.2 us (4%)
    all_gather x1, waiting for transfers between devices, reduce_gradients(): return jnp.sum(lax.all_gather(partial_sum, 'bucket'), axis=0)  98.9 us
    scatter-add x2, other arithmetic, edge_targets(): table.at[edge_slot, edge_left, edge_right]  62.7 us
    reduce_scatter x1, waiting for transfers between devices, reduce_gradients(): lax.psum_scatter(term.reshape(rel_count_piece * width, width), 'rel', sca...  43.2 us
    all_gather x1, waiting for transfers between devices, partner_blocks(): lax.all_gather(row_block, 'bucket', axis=0, tiled=True)  34.1 us
    all_gather x1, blocking collectives, partner_blocks(): lax.all_gather(state_block, 'bucket', axis=0, tiled=True)  21.1 us
  transfers between devices with their start and end apart: 4, of which 3 were waited for; matrix products, arithmetic and copies ran while one was open for 25% of the time, Pallas kernels for 0%

profile of v1, /device:TPU:0, one launch (start us, length us, event | category | flops | bytes accessed | tf_op | source)
XLA Modules:
  0.0 329.0 jit_solution(6200558762393507346)
XLA Ops:
  7.2 0.7 all-gather.6.cloned.1.call-update
  8.0 1.1 convert_element_type.63
  9.0 1.1 convert_element_type.65
  10.1 0.8 slice_convert_fusion
  10.9 0.8 or_select_fusion
  11.7 31.3 %scatter_fusion = f32[2,256,256]{2,1,0:T(8,128)S(1)} fusion(f32[2,256,256]{2,1,0:T(8,128)S(1)} %broadcast.145.clone, s32[512]{0:T(512)S(1)} %bitcast.127, f32[512]{0:T(512)S(1)} %bitcast.133), kind=kCustom, calls=%fused_computation.2 | custom fusion | flops 512 | bytes 12288 | tf_op jit(solution)/shard_map/scatter-add | solution.py:11
  43.1 0.6 compare_and_fusion
  43.7 2.2 gather_fusion
  48.0 0.6 fusion.39
  48.6 0.9 divide_subtract_fusion.2
  50.5 31.3 %scatter_fusion.1 = f32[2,256,256]{2,1,0:T(8,128)S(1)} fusion(f32[2,256,256]{2,1,0:T(8,128)S(1)} %broadcast.145.clone.1, s32[512]{0:T(512)S(1)} %bitcast.126, f32[512]{0:T(512)S(1)} %bitcast.132), kind=kCustom, calls=%fused_computation.3 | custom fusion | flops 512 | bytes 12288 | tf_op jit(solution)/shard_map/scatter-add | solution.py:11
  81.8 0.6 iota_compare_fusion.1
  82.4 3.2 gather_fusion.1
  85.8 1.3 convolution_bitcast_fusion.2
  87.3 1.3 convolution_bitcast_fusion.3
  90.1 1.0 convolution_convert_fusion.1
  91.1 34.1 %all-gather.8.cloned.1.call-done = f32[2048,512]{1,0:T(8,128)} async-done(((f32[256,512]{1,0:T(8,128)}), f32[2048,512]{1,0:T(8,128)}) %all-gather.8.cloned.1.call-update) | async-done | bytes 4194320 | tf_op jit(solution)/shard_map/all_gather | solution.py:65
  125.2 2.9 select_reduce_fusion
  130.0 2.4 pad_maximum_fusion
  132.4 5.5 %copy.25 = f32[4,512,512]{2,0,1:T(4,128)} copy(f32[4,512,512]{1,2,0:T(8,128)} %pad_maximum_fusion) | data formatting | bytes 8388608 | tf_op jit(solution)/shard_map/stack | solution.py:79
  137.8 6.2 %fusion.32 = f32[4,512,512]{2,0,1:T(4,128)S(1)} fusion(f32[4,512,512]{2,0,1:T(4,128)} %copy.25, s32[4]{0:T(128)S(1)} %bitcast.134), kind=kOutput, calls=%fused_computation.98 | convolution fusion | flops 50331664 | bytes 8388624 | tf_op jit(solution)/shard_map/sk,sde->kde/dot_general | solution.py:84
  144.0 3.2 copy.26
  147.4 43.2 %reduce-scatter.2.cloned.1.call-done = f32[512,512]{1,0:T(8,128)} async-done(((f32[2048,512]{1,0:T(8,128)}), f32[512,512]{1,0:T(8,128)}) %reduce-scatter.2.cloned.1.call-update) | async-done | bytes 1048592 | tf_op jit(solution)/shard_map/reduce_scatter | solution.py:85
  190.6 21.1 %all-gather.1 = f32[8,1,256]{2,1,0:T(1,128)S(1)} all-gather(f32[1,1,256]{2,1,0:T(1,128)S(1)} %bitcast.135), channel_id=1, replica_groups=mesh['bucket'=8,'rel'=4] {'bucket'}, dimensions={0}, use_global_device_ids=true | all-gather | bytes 9216 | tf_op jit(solution)/shard_map/all_gather | solution.py:66
  211.8 1.2 fusion.41
  213.0 1.3 multiply_reduce_fusion
  214.3 0.6 fusion.37
  215.6 0.6 fusion.38
  216.2 0.9 divide_subtract_fusion
  217.1 1.0 divide_subtract_fusion.1
  218.1 98.9 %all-gather.10.cloned.1.call-done = f32[4096,512]{1,0:T(8,128)} async-done(((f32[512,512]{1,0:T(8,128)}), f32[4096,512]{1,0:T(8,128)}) %all-gather.10.cloned.1.call-update) | async-done | bytes 8388624 | tf_op jit(solution)/shard_map/all_gather | solution.py:88
  317.1 5.5 %reduce_sum.69 = f32[512,512]{1,0:T(8,128)} reduce(f32[8,512,512]{2,1,0:T(8,128)} %bitcast.129, f32[]{:T(128)} %constant.15.clone.1), dimensions={0}, to_apply=%region_9.11 | reduce | flops 1835008 | bytes 9437188 | tf_op jit(solution)/shard_map/reduce_sum | solution.py:88
  (72 shorter events, 7.0 us)
Async XLA Ops:
  7.2 35.9 %copy-start.11 = (s32[1,1,4]{2,1,0:T(1,128)S(1)}, s32[1,1,4]{2,1,0:T(1,128)}, u32[]{:S(2)}) copy-start(s32[1,1,4]{2,1,0:T(1,128)} %param.18) | copy-start | bytes 52
  7.2 36.5 %all-gather.6.cloned.1.call-start = ((), (), s32[]{:S(2)}) async-start(), calls=%async_computation.1 | async-start | bytes 2621440 | tf_op jit(solution)/shard_map/all_gather | solution.py:105
  7.9 117.3 %all-gather.8.cloned.1.call-start = ((), (), s32[]{:S(2)}) async-start(), calls=%async_computation.2 | async-start | bytes 4718592 | tf_op jit(solution)/shard_map/all_gather | solution.py:65
  46.1 2.0 copy-start.17
  46.1 2.5 copy-start.6
  49.6 141.0 %reduce-scatter.2.cloned.1.call-start = ((), (), s32[]{:S(2)}) async-start(), calls=%async_computation.3 | async-start | bytes 5242880 | tf_op jit(solution)/shard_map/reduce_scatter | solution.py:85
  85.6 3.9 %copy-start.12 = (f32[256]{0:T(256)S(1)}, f32[256]{0:T(256)}, u32[]{:S(2)}) copy-start(f32[256]{0:T(256)} %param.14) | copy-start | bytes 3076
  85.6 3.9 %copy-start = (f32[256,512]{1,0:T(8,128)S(1)}, f32[256,512]{1,0:T(8,128)}, u32[]{:S(2)}) copy-start(f32[256,512]{1,0:T(8,128)} %param.13) | copy-start | bytes 1572868
  85.8 3.8 %copy-start.1 = (bf16[2,512,512]{2,1,0:T(8,128)(2,1)S(1)}, bf16[2,512,512]{2,1,0:T(8,128)(2,1)}, u32[]{:S(2)}) copy-start(bf16[2,512,512]{2,1,0:T(8,128)(2,1)} %gather_fusion.1) | copy-start | bytes 3145732
  85.8 3.8 %copy-start.16 = (pred[2]{0:T(512)(128)(4,1)S(1)}, pred[2]{0:T(512)(128)(4,1)}, u32[]{:S(2)}) copy-start(pred[2]{0:T(512)(128)(4,1)} %get-tuple-element.12) | copy-start | bytes 10
  88.7 36.5 %copy-start.14 = (pred[8]{0:T(512)(128)(4,1)S(1)}, pred[8]{0:T(512)(128)(4,1)}, u32[]{:S(2)}) copy-start(pred[8]{0:T(512)(128)(4,1)} %iota_compare_fusion.1) | copy-start | bytes 28
  89.6 35.6 %copy-start.4 = (bf16[256,512]{1,0:T(8,128)(2,1)}, bf16[256,512]{1,0:T(8,128)(2,1)S(1)}, u32[]{:S(2)}) copy-start(bf16[256,512]{1,0:T(8,128)(2,1)S(1)} %fusion.36) | copy-start | bytes 786436
  90.1 38.0 %copy-start.10 = (bf16[256,512]{1,0:T(8,128)(2,1)}, bf16[256,512]{1,0:T(8,128)(2,1)S(1)}, u32[]{:S(2)}) copy-start(bf16[256,512]{1,0:T(8,128)(2,1)S(1)} %convolution_convert_fusion.3) | copy-start | bytes 786436
  125.2 3.5 %copy-start.9 = (bf16[256,512]{1,0:T(8,128)(2,1)S(1)}, bf16[256,512]{1,0:T(8,128)(2,1)}, u32[]{:S(2)}) copy-start(bf16[256,512]{1,0:T(8,128)(2,1)} %convolution_convert_fusion.1) | copy-start | bytes 786436
  125.2 4.0 %copy-start.5 = (bf16[256,512]{1,0:T(8,128)(2,1)S(1)}, bf16[256,512]{1,0:T(8,128)(2,1)}, u32[]{:S(2)}) copy-start(bf16[256,512]{1,0:T(8,128)(2,1)} %copy-done.4) | copy-start | bytes 786436
  128.1 1.9 copy-start.2
  128.1 1.9 copy-start.3
  128.4 0.8 copy-start.7
  147.3 43.3 %copy-start.13 = (f32[256]{0:T(256)S(1)}, f32[256]{0:T(256)}, u32[]{:S(2)}) copy-start(f32[256]{0:T(256)} %get-tuple-element.11) | copy-start | bytes 3076
  147.3 64.4 %copy-start.15 = (pred[8]{0:T(512)(128)(4,1)S(1)}, pred[8]{0:T(512)(128)(4,1)}, u32[]{:S(2)}) copy-start(pred[8]{0:T(512)(128)(4,1)} %iota_compare_fusion.1) | copy-start | bytes 28
  147.3 64.5 %copy-start.8 = (bf16[256,256]{1,0:T(8,128)(2,1)S(1)}, bf16[256,256]{1,0:T(8,128)(2,1)}, u32[]{:S(2)}) copy-start(bf16[256,256]{1,0:T(8,128)(2,1)} %copy-done.7) | copy-start | bytes 393220
  147.3 169.8 %all-gather.10.cloned.1.call-start = ((), (), s32[]{:S(2)}) async-start(), calls=%async_computation.4 | async-start | bytes 9437184 | tf_op jit(solution)/shard_map/all_gather | solution.py:88
Sparse Core Ops, SparseCore 0:
  9.5 25.2 all-gather.5
  49.7 75.4 all-gather.7
  147.4 43.0 reduce-scatter.1
  192.5 124.4 all-gather.9
